TPU v7x, 256 devices: a whole 4x4x8 slice. The times are simulated.
256 devices in a mesh: seq: 8 (over z_lo, core), blk: 32 (over y, z_hi, x).
Axes of the slice: x: 4, y: 4, z: 8 (z_hi: 2, z_lo: 4; z = z_hi * 4 + z_lo), core: 2. Of those that a mesh axis runs over, the one named last changes fastest.
Arguments:
- stream: float32 [4096, 3072], P(('seq', 'blk')), may hold values from -39 to 39
- key_keep: int32 [4096], replicated, may hold values 0 or 1
- positions: int32 [4096, 3], replicated, may hold values from 0 to 63
- lengths: int32 [4], replicated, may hold values from 1 to 2048, 4096 in all
- step_index: int32 [4], replicated, may hold values from 0 to 27
- mod_table: bfloat16 [4, 28, 3, 3072], replicated, may hold values from -4 to 4
- w_qkv: bfloat16 [3072, 9216], P(None, 'blk'), may hold values from -0.109375 to 0.109375
- w_mlp_in: bfloat16 [3072, 12288], P(None, 'blk'), may hold values from -0.109375 to 0.109375
- q_gain: float32 [128], replicated, may hold values from 0.5 to 10
- k_gain: float32 [128], replicated, may hold values from 0.5 to 10
- w_attn_out: bfloat16 [3072, 3072], P('blk'), may hold values from -0.109375 to 0.109375
- w_mlp_out: bfloat16 [12288, 3072], P('blk'), may hold values from -0.0546875 to 0.0546875
Outputs:
- stream_next: float32 [4096, 3072], P(('seq', 'blk'))
Inputs may be any that keep to these rules, and one draw needn't show every extreme that they name: The lengths sum to 4096; the longest request has exactly 2048 tokens.
All inputs are finite; a program needn't handle non-finite values.
Results may differ from a plain program's by a relative error of at most 0.0082.
The roundings to bfloat16 on the way count: a program that leaves them out, or rounds other values in their place, can miss the bound.
Values may be sent and summed in bfloat16 or wider, within the bound.
No kernel may reach another device: no remote copies, remote signals or barrier semaphores. Data moves between devices by JAX's collectives and lax.ppermute only.
A program may use at most 64 MiB of HBM per device.

v0:
```python
import math
import jax
import jax.numpy as jnp
from jax import lax
from jax.sharding import PartitionSpec as P


def rope_table(head_size):
    first_count = head_size // 16
    second = 7 * head_size // 32
    pair_ids = jnp.arange(head_size // 2, dtype=jnp.int32)
    pair_axis = jnp.where(
        pair_ids < first_count, 0, jnp.where(pair_ids < first_count + second, 1, 2)
    )
    pair_local = jnp.where(
        pair_ids < first_count,
        pair_ids,
        jnp.where(
            pair_ids < first_count + second, pair_ids - first_count, pair_ids - first_count - second
        ),
    )
    axis_dims = jnp.where(pair_axis == 0, 2 * first_count, 2 * second)
    frequency = jnp.power(
        jnp.float32(10000.0), -(2 * pair_local).astype(jnp.float32) / axis_dims.astype(jnp.float32)
    )
    return jnp.where(
        jnp.arange(3)[:, None] == pair_axis[None, :], frequency[None, :], jnp.float32(0.0)
    )


def angles_of(places, freq_table):
    return jnp.sum(places.astype(jnp.float32)[:, :, None] * freq_table[None, :, :], axis=1)


def rotate(values, angles):
    paired = values.reshape(values.shape[:-1] + (values.shape[-1] // 2, 2))
    even_part = paired[..., 0]
    odd_part = paired[..., 1]
    cos_part = jnp.cos(angles)[:, None, :]
    sin_part = jnp.sin(angles)[:, None, :]
    turned = jnp.stack(
        [cos_part * even_part - sin_part * odd_part, sin_part * even_part + cos_part * odd_part],
        axis=-1,
    )
    return turned.reshape(values.shape)


def rms_scale(values, gain_vec):
    return values * lax.rsqrt(jnp.mean(values * values, axis=-1, keepdims=True) + 1e-06) * gain_vec


def segment_of(row_ids, request_ends):
    return jnp.sum((row_ids[:, None] >= request_ends[None, :]).astype(jnp.int32), axis=1)


def spread_rows(row_ids, query_rows, block_rows, tok_seq):
    owner = row_ids // query_rows
    within = row_ids % query_rows
    return within // block_rows * tok_seq + owner * block_rows + within % block_rows


def body(
    stream,
    key_keep,
    positions,
    lengths,
    step_index,
    mod_table,
    w_qkv,
    w_mlp_in,
    q_gain,
    k_gain,
    w_attn_out,
    w_mlp_out,
):
    blk_count = lax.axis_size("blk")
    seq_count = lax.axis_size("seq")
    seq_at = lax.axis_index("seq")
    blk_at = lax.axis_index("blk")
    block_rows = stream.shape[0]
    width = stream.shape[1]
    tok_seq = block_rows * blk_count
    head_size = q_gain.shape[0]
    local_heads = width // head_size // seq_count
    requests = mod_table.shape[0]
    step_total = mod_table.shape[1]
    inv_root = 1.0 / math.sqrt(head_size)
    request_ends = jnp.cumsum(lengths)
    own_rows = seq_at * tok_seq + blk_at * block_rows + jnp.arange(block_rows, dtype=jnp.int32)
    own_request = segment_of(own_rows, request_ends)
    step_pick = (jnp.arange(step_total, dtype=jnp.int32)[None, :] == step_index[:, None]).astype(
        jnp.bfloat16
    )
    modulation = jnp.einsum(
        "rs,rsk->rk",
        step_pick,
        mod_table.reshape(requests, step_total, 3 * width),
        preferred_element_type=jnp.float32,
    )
    member = (own_request[:, None] == jnp.arange(requests, dtype=jnp.int32)[None, :]).astype(
        jnp.float32
    )
    token_mod = jnp.dot(member, modulation, precision=lax.Precision.HIGHEST)
    mod_shift = token_mod[:, :width]
    mod_scale = token_mod[:, width : 2 * width]
    mod_gate = token_mod[:, 2 * width :]
    row_mean = jnp.mean(stream, axis=1, keepdims=True)
    centered = stream - row_mean
    row_var = jnp.mean(centered * centered, axis=1, keepdims=True)
    normed = centered * lax.rsqrt(row_var + 1e-06)
    modin = ((1.0 + mod_scale) * normed + mod_shift).astype(jnp.bfloat16)
    qkv_width = w_qkv.shape[1]
    shard_rows = lax.all_gather(modin, "blk", axis=0, tiled=True)
    qkv_part = jnp.dot(shard_rows, w_qkv, preferred_element_type=jnp.float32).astype(jnp.bfloat16)
    mlp_part = jax.nn.gelu(
        jnp.dot(shard_rows, w_mlp_in, preferred_element_type=jnp.float32), approximate=True
    ).astype(jnp.bfloat16)
    joined = jnp.concatenate([qkv_part, mlp_part], axis=1)
    qkv_cols = joined[:, :qkv_width]
    mlp_act = joined[:, qkv_width:]
    heads_in = lax.all_to_all(
        lax.all_to_all(qkv_cols, "blk", split_axis=0, concat_axis=1, tiled=True),
        "seq",
        split_axis=1,
        concat_axis=0,
        tiled=True,
    )
    query_rows = heads_in.shape[0]
    heads4 = heads_in.reshape(query_rows, local_heads, 3, head_size)
    query_ids = spread_rows(
        blk_at * query_rows + jnp.arange(query_rows, dtype=jnp.int32),
        query_rows,
        block_rows,
        tok_seq,
    )
    query_request = segment_of(query_ids, request_ends)
    angles = angles_of(jnp.take(positions, query_ids, axis=0), rope_table(head_size))
    query_rot = rotate(rms_scale(heads4[:, :, 0].astype(jnp.float32), q_gain), angles).astype(
        jnp.bfloat16
    )
    key_rot = rotate(rms_scale(heads4[:, :, 1].astype(jnp.float32), k_gain), angles).astype(
        jnp.bfloat16
    )
    value_rows = heads4[:, :, 2]
    run_top = jnp.full((query_rows, local_heads), -1e30, jnp.float32)
    key_part = lax.all_gather(key_rot, "blk", axis=0, tiled=True)
    value_part = lax.all_gather(value_rows, "blk", axis=0, tiled=True)
    key_ids = spread_rows(
        jnp.arange(key_part.shape[0], dtype=jnp.int32), query_rows, block_rows, tok_seq
    )
    key_request = segment_of(key_ids, request_ends)
    kept = jnp.take(key_keep, key_ids) == 1
    visible = (
        (query_request[:, None] == key_request[None, :])
        & (kept[None, :] | (query_ids[:, None] == key_ids[None, :]))
    )[:, None, :]
    scores = (
        jnp.einsum("qhd,khd->qhk", query_rot, key_part, preferred_element_type=jnp.float32)
        * inv_root
    )
    row_high = jnp.max(jnp.where(visible, scores, -1e30), axis=2)
    new_top = jnp.maximum(run_top, row_high)
    weights = jnp.where(visible, jnp.exp(scores - new_top[:, :, None]), 0.0)
    run_norm = jnp.sum(weights, axis=2)
    run_sum = jnp.einsum(
        "qhk,khd->qhd", weights.astype(jnp.bfloat16), value_part, preferred_element_type=jnp.float32
    )
    run_top, run_norm, run_sum = (new_top, run_norm, run_sum)
    attended = (run_sum / run_norm[:, :, None]).astype(jnp.bfloat16)
    attended = attended.reshape(query_rows, local_heads * head_size)
    attn_local = lax.all_to_all(
        lax.all_to_all(attended, "seq", split_axis=0, concat_axis=1, tiled=True),
        "blk",
        split_axis=1,
        concat_axis=0,
        tiled=True,
    )
    mlp_part = mlp_act
    summed = lax.psum_scatter(
        (
            jnp.dot(attn_local, w_attn_out, preferred_element_type=jnp.float32)
            + jnp.dot(mlp_part, w_mlp_out, preferred_element_type=jnp.float32)
        ).astype(jnp.bfloat16),
        "blk",
        scatter_dimension=0,
        tiled=True,
    ).astype(jnp.float32)
    return stream + mod_gate * summed


def solution(mesh):
    in_specs = (
        P(("seq", "blk"), None),
        P(),
        P(),
        P(),
        P(),
        P(),
        P(None, "blk"),
        P(None, "blk"),
        P(),
        P(),
        P("blk", None),
        P("blk", None),
    )
    out_specs = P(("seq", "blk"), None)
    return jax.shard_map(body, mesh=mesh, in_specs=in_specs, out_specs=out_specs, check_vma=False)
```

profile of v0, /device:TPU:2, one launch (start us, length us, event | category | flops | bytes accessed | tf_op | source)
XLA Modules:
  0.0 693.5 jit_solution(4572374142016408520)
XLA Ops:
  7.5 1.1 reduce_sum.82
  8.5 1.1 multiply_reduce_fusion.2
  10.6 2.8 fusion.11
  14.7 102.6 %all-gather.5.cloned.1.call-done = bf16[512,3072]{1,0:T(8,128)(2,1)} async-done(((bf16[16,3072]{1,0:T(8,128)(2,1)}), bf16[512,3072]{1,0:T(8,128)(2,1)}) %all-gather.5.cloned.1.call-update) | async-done | bytes 3145744 | tf_op jit(solution)/shard_map/all_gather | solution.py:113
  117.3 3.5 convolution_convert_fusion
  121.8 6.2 all-to-all-start
  129.5 2.8 copy.83
  132.3 2.8 gather_fusion.1
  136.7 5.6 all-to-all-done
  143.1 1.5 all_to_all.53
  145.3 3.9 all-to-all-start.1
  150.8 8.9 %all-to-all-done.1 = bf16[16,8,1152]{2,0,1:T(8,128)(2,1)S(1)} async-done(((bf16[16,8,1152]{2,0,1:T(8,128)(2,1)}), bf16[16,8,1152]{2,0,1:T(8,128)(2,1)S(1)}, u32[]{:S(2)}, u32[]{:S(2)}) %all-to-all-start.1) | async-done | bytes 294944 | tf_op jit(solution)/shard_map/all_to_all | solution.py:121
  161.4 1.1 fusion.86
  164.5 1.7 copy.86
  166.2 1.3 add_rsqrt_fusion
  168.3 1.1 multiply_multiply_fusion.2
  169.4 1.1 multiply_multiply_fusion.1
  170.5 2.0 subtract_convert_fusion
  174.7 23.0 %gather_fusion = s32[4096]{0:T(1024)S(1)} fusion(s32[4096]{0:T(1024)S(1)} %copy-done.1, s32[4096]{0:T(1024)S(1)} %broadcast_clamp_fusion), kind=kCustom, calls=%fused_computation | custom fusion | bytes 49152 | tf_op jit(solution)/shard_map/jit(_take)/gather | solution.py:152
  198.0 4.5 or_and_fusion
  202.8 66.0 %all-gather.7.cloned.1.call-done = bf16[4096,3,128]{2,0,1:T(8,128)(2,1)} async-done(((bf16[128,3,128]{2,0,1:T(8,128)(2,1)}), bf16[4096,3,128]{2,0,1:T(8,128)(2,1)}) %all-gather.7.cloned.1.call-update) | async-done | bytes 3145744 | tf_op jit(solution)/shard_map/all_gather | solution.py:146
  268.8 3.2 fusion
  272.1 2.6 copy-done.2
  274.7 1.2 fusion.3
  275.9 106.2 %all-gather.9.cloned.1.call-done = bf16[4096,3,1,128]{0,3,1,2:T(8,128)(2,1)} async-done(((bf16[128,3,1,128]{0,3,1,2:T(8,128)(2,1)}), bf16[4096,3,1,128]{0,3,1,2:T(8,128)(2,1)}) %all-gather.9.cloned.1.call-update) | async-done | bytes 3145744 | tf_op jit(solution)/shard_map/all_gather | solution.py:147
  382.1 5.3 fusion.23
  387.7 8.7 %all_to_all.67 = bf16[8,16,384]{2,1,0:T(8,128)(2,1)S(1)} all-to-all(bf16[8,16,384]{2,1,0:T(8,128)(2,1)S(1)} %all_to_all.56), channel_id=1, replica_groups=mesh['seq'=8,'blk'=32] {'seq'}, dimensions={0} | all-to-all | bytes 196608 | tf_op jit(solution)/shard_map/all_to_all | solution.py:172
  396.6 19.6 %all_to_all.68 = bf16[16,32,96]{2,0,1:T(8,128)(2,1)S(1)} all-to-all(bf16[16,32,96]{2,0,1:T(8,128)(2,1)S(1)} %copy.98), channel_id=1, replica_groups=mesh['seq'=8,'blk'=32] {'blk'}, dimensions={1} | all-to-all | bytes 196608 | tf_op jit(solution)/shard_map/all_to_all | solution.py:171
  416.2 4.7 fusion.90
  420.9 9.6 %add_convert_fusion = bf16[512,3072]{1,0:T(8,128)(2,1)} fusion(f32[512,3072]{1,0:T(8,128)} %fusion.90, bf16[384,3072]{1,0:T(8,128)(2,1)S(1)} %copy-done, bf16[512,3072]{1,0:T(8,128)(2,1)} %all-gather.5.cloned.1.call-done, bf16[3072,384]{1,0:T(8,128)(2,1)} %param.19), kind=kOutput, calls=%fused_computation.7 | convolution fusion | flops 2420834304 | bytes 17301504 | tf_op jit(solution)/shard_map/dot_general | solution.py:182
  430.5 254.9 %reduce-scatter.2.cloned.1.call-done = bf16[16,3072]{1,0:T(8,128)(2,1)} async-done(((bf16[512,3072]{1,0:T(8,128)(2,1)}), bf16[16,3072]{1,0:T(8,128)(2,1)}) %reduce-scatter.2.cloned.1.call-update) | async-done | bytes 98320 | tf_op jit(solution)/shard_map/reduce_scatter | solution.py:179
  685.4 1.6 fusion.43
  (78 shorter events, 17.8 us)
Async XLA Ops:
  6.5 414.4 %copy-start = (bf16[384,3072]{1,0:T(8,128)(2,1)S(1)}, bf16[384,3072]{1,0:T(8,128)(2,1)}, u32[]{:S(2)}) copy-start(bf16[384,3072]{1,0:T(8,128)(2,1)} %param.23) | copy-start | bytes 7077892
  6.5 7.3 %copy-start.3 = (f32[16,3072]{1,0:T(8,128)S(1)}, f32[16,3072]{1,0:T(8,128)}, u32[]{:S(2)}) copy-start(f32[16,3072]{1,0:T(8,128)} %param.12) | copy-start | bytes 589828
  6.5 110.8 %all-gather.5.cloned.1.call-start = ((), (), s32[]{:S(2)}) async-start(), calls=%async_computation.5 | async-start | bytes 3244032 | tf_op jit(solution)/shard_map/all_gather | solution.py:113
  10.5 4.2 copy-start.11
  14.7 113.3 %copy-start.9 = (f32[128]{0:T(128)S(1)}, f32[128]{0:T(128)}, u32[]{:S(2)}) copy-start(f32[128]{0:T(128)} %param.21) | copy-start | bytes 1540
  14.7 114.1 %copy-start.10 = (f32[128]{0:T(128)S(1)}, f32[128]{0:T(128)}, u32[]{:S(2)}) copy-start(f32[128]{0:T(128)} %param.20) | copy-start | bytes 1540
  121.8 20.5 %all-to-all-start = ((bf16[32,16,288]{2,1,0:T(8,128)(2,1)}), bf16[32,16,288]{2,1,0:T(8,128)(2,1)S(1)}, u32[]{:S(2)}, u32[]{:S(2)}) async-start(bf16[32,16,288]{2,1,0:T(8,128)(2,1)} %bitcast.68), calls=%async_computation | async-start | bytes 786432 | tf_op jit(solution)/shard_map/all_to_all | solution.py:122
  145.3 14.3 %all-to-all-start.1 = ((bf16[16,8,1152]{2,0,1:T(8,128)(2,1)}), bf16[16,8,1152]{2,0,1:T(8,128)(2,1)S(1)}, u32[]{:S(2)}, u32[]{:S(2)}) async-start(bf16[16,8,1152]{2,0,1:T(8,128)(2,1)} %copy.81), calls=%async_computation.1 | async-start | bytes 589824 | tf_op jit(solution)/shard_map/all_to_all | solution.py:121
  149.2 119.6 %all-gather.7.cloned.1.call-start = ((), (), s32[]{:S(2)}) async-start(), calls=%async_computation.6 | async-start | bytes 3244032 | tf_op jit(solution)/shard_map/all_gather | solution.py:146
  159.6 0.7 copy-start.5
  160.3 14.3 %copy-start.1 = (s32[4096]{0:T(1024)S(1)}, s32[4096]{0:T(1024)}, u32[]{:S(2)}) copy-start(s32[4096]{0:T(1024)} %param.13) | copy-start | bytes 49156
  162.5 11.0 %copy-start.6 = (bf16[128,3,1,128]{3,2,1,0:T(2,128)(2,1)S(1)}, bf16[128,3,1,128]{3,2,1,0:T(2,128)(2,1)}, u32[]{:S(2)}) copy-start(bf16[128,3,1,128]{3,2,1,0:T(2,128)(2,1)} %get-tuple-element.5) | copy-start | bytes 294916
  173.5 208.7 %all-gather.9.cloned.1.call-start = ((), (), s32[]{:S(2)}) async-start(), calls=%async_computation.8 | async-start | bytes 3244032 | tf_op jit(solution)/shard_map/all_gather | solution.py:147
  174.3 511.1 %reduce-scatter.2.cloned.1.call-start = ((), (), s32[]{:S(2)}) async-start(), calls=%async_computation.7 | async-start | bytes 3244032 | tf_op jit(solution)/shard_map/reduce_scatter | solution.py:179
  174.7 23.1 %copy-start.12 = (s32[4,1]{0,1:T(1,128)S(1)}, s32[4,1]{0,1:T(1,128)}, u32[]{:S(2)}) copy-start(s32[4,1]{0,1:T(1,128)} %copy-done.11) | copy-start | bytes 52
  174.7 27.9 %copy-start.7 = (bf16[128,3,64,1]{0,3,2,1:T(2,128)(2,1)S(1)}, bf16[128,3,64,1]{0,3,2,1:T(2,128)(2,1)}, u32[]{:S(2)}) copy-start(bf16[128,3,64,1]{0,3,2,1:T(2,128)(2,1)} %get-tuple-element.8) | copy-start | bytes 147460
  174.7 27.9 %copy-start.8 = (bf16[128,3,64,1]{0,3,2,1:T(2,128)(2,1)S(1)}, bf16[128,3,64,1]{0,3,2,1:T(2,128)(2,1)}, u32[]{:S(2)}) copy-start(bf16[128,3,64,1]{0,3,2,1:T(2,128)(2,1)} %get-tuple-element.9) | copy-start | bytes 147460
  268.8 5.9 copy-start.4
  272.0 2.7 copy-start.2
Sparse Core Ops, SparseCore 0:
  14.8 102.5 all-gather.4
  173.6 95.2 all-gather.6
  272.0 110.0 all-gather.8
  430.6 254.7 reduce-scatter.1
where the time goes:
time: 694 us
  waiting for transfers between devices  544 us (78%)
  local copies, waits for them, and re-layouts  45.8 us (7%)
  matrix products  29.6 us (4%)
  blocking collectives  28.3 us (4%)
  other arithmetic  21.7 us (3%)
  between operations  13.4 us (2%)
  starting transfers between devices  10.4 us (1%)
    reduce_scatter x1, waiting for transfers between devices, body(): lax.psum_scatter((jnp.dot(attn_local, w_attn_out, preferred_element_type=...  255 us
    all_gather x1, waiting for transfers between devices, body(): value_part = lax.all_gather(value_rows, 'blk', axis=0, tiled=True)  106 us
    all_gather x1, waiting for transfers between devices, body(): shard_rows = lax.all_gather(modin, 'blk', axis=0, tiled=True)  103 us
    all_gather x1, waiting for transfers between devices, body(): key_part = lax.all_gather(key_rot, 'blk', axis=0, tiled=True)  66 us
    gather x1, local copies, waits for them, and re-layouts, body(): kept = jnp.take(key_keep, key_ids) == 1  23 us
    all_to_all x1, blocking collectives, body(): lax.all_to_all(lax.all_to_all(attended, 'seq', split_axis=0, concat_axis=...  19.6 us
  transfers between devices with their start and end apart: 6, of which 6 were waited for; matrix products, arithmetic and copies ran while one was open for 6% of the time, Pallas kernels for 0%

commit v1 on v0

--- a/solution.py
+++ b/solution.py
@@ -143,7 +143,10 @@
     )
     value_rows = heads4[:, :, 2]
     run_top = jnp.full((query_rows, local_heads), -1e30, jnp.float32)
-    key_part = lax.all_gather(key_rot, "blk", axis=0, tiled=True)
+    key_part = jnp.concatenate(
+        lax.all_to_all(jnp.stack([key_rot for _ in range(lax.axis_size("blk"))]), "blk", 0, 0),
+        axis=0,
+    )
     value_part = lax.all_gather(value_rows, "blk", axis=0, tiled=True)
     key_ids = spread_rows(
         jnp.arange(key_part.shape[0], dtype=jnp.int32), query_rows, block_rows, tok_seq

time: 694 us -> 638 us (0.919)
  waiting for transfers between devices: 544 us -> 483 us
    all_gather x1 -> x0, waiting for transfers between devices: 66 us -> none  [body(): key_part = lax.all_gather(key_rot, 'blk', axis=0, tiled=True)]
    all_to_all x0 -> x1, waiting for transfers between devices: none -> 49.1 us  [body(): lax.all_to_all(jnp.stack([key_rot for _ in range(lax.axis_size('blk'))]),...]
    all_gather x1, waiting for transfers between devices: 106 us -> 61.4 us  [body(): value_part = lax.all_gather(value_rows, 'blk', axis=0, tiled=True)]
  transfers between devices with their start and end apart: 6 -> 6, of which waited for: 6 -> 6; matrix products, arithmetic and copies ran while one was open for 6% -> 7% of each run, Pallas kernels for 0% -> 0%
where the time goes in v1:
time: 638 us; the launch traced here: 637 us
  waiting for transfers between devices  483 us (76%)
  local copies, waits for them, and re-layouts  49.3 us (8%)
  blocking collectives  28.3 us (4%)
  matrix products  27.6 us (4%)
  other arithmetic  19.1 us (3%)
  starting transfers between devices  16.8 us (3%)
  between operations  13.4 us (2%)
    reduce_scatter x1, waiting for transfers between devices, body(): lax.psum_scatter((jnp.dot(attn_local, w_attn_out, preferred_element_type=...  255 us
    all_gather x1, waiting for transfers between devices, body(): shard_rows = lax.all_gather(modin, 'blk', axis=0, tiled=True)  103 us
    all_gather x1, waiting for transfers between devices, body(): value_part = lax.all_gather(value_rows, 'blk', axis=0, tiled=True)  61.4 us
    all_to_all x1, waiting for transfers between devices, body(): lax.all_to_all(jnp.stack([key_rot for _ in range(lax.axis_size('blk'))]),...  49.1 us
    gather x1, local copies, waits for them, and re-layouts, body(): kept = jnp.take(key_keep, key_ids) == 1  23 us
    all_to_all x1, blocking collectives, body(): lax.all_to_all(lax.all_to_all(attended, 'seq', split_axis=0, concat_axis=...  19.6 us
  transfers between devices with their start and end apart: 6, of which 6 were waited for; matrix products, arithmetic and copies ran while one was open for 7% of the time, Pallas kernels for 0%

profile of v1, /device:TPU:2, one launch (start us, length us, event | category | flops | bytes accessed | tf_op | source)
XLA Modules:
  0.0 637.2 jit_solution(6468055761476219795)
XLA Ops:
  7.5 1.1 reduce_sum.82
  8.5 1.1 multiply_reduce_fusion.2
  10.6 2.8 fusion.11
  14.7 102.6 %all-gather.4.cloned.1.call-done = bf16[512,3072]{1,0:T(8,128)(2,1)} async-done(((bf16[16,3072]{1,0:T(8,128)(2,1)}), bf16[512,3072]{1,0:T(8,128)(2,1)}) %all-gather.4.cloned.1.call-update) | async-done | bytes 3145744 | tf_op jit(solution)/shard_map/all_gather | solution.py:113
  117.3 3.5 convolution_convert_fusion
  121.8 6.2 all-to-all-start
  129.5 2.8 copy.85
  132.3 2.8 gather_fusion.1
  136.7 5.6 all-to-all-done
  143.1 1.5 all_to_all.56
  145.3 3.9 all-to-all-start.1
  150.7 8.9 %all-to-all-done.1 = bf16[16,8,1152]{2,0,1:T(8,128)(2,1)S(1)} async-done(((bf16[16,8,1152]{2,0,1:T(8,128)(2,1)}), bf16[16,8,1152]{2,0,1:T(8,128)(2,1)S(1)}, u32[]{:S(2)}, u32[]{:S(2)}) %all-to-all-start.1) | async-done | bytes 294944 | tf_op jit(solution)/shard_map/all_to_all | solution.py:121
  161.4 1.1 fusion.86
  166.1 1.1 multiply_multiply_fusion.1
  167.2 2.0 subtract_convert_fusion
  169.5 2.5 stack.9
  172.0 6.5 %all-to-all-start.2 = ((bf16[32,128,3,128]{3,1,2,0:T(8,128)(2,1)}), bf16[32,128,3,128]{3,1,2,0:T(8,128)(2,1)}, u32[]{:S(2)}, u32[]{:S(2)}) async-start(bf16[32,128,3,128]{3,1,2,0:T(8,128)(2,1)} %stack.9), calls=%async_computation.2 | async-start | bytes 6291456 | tf_op jit(solution)/shard_map/all_to_all | solution.py:147
  179.8 23.0 %gather_fusion = s32[4096]{0:T(1024)S(1)} fusion(s32[4096]{0:T(1024)S(1)} %copy-done.1, s32[4096]{0:T(1024)S(1)} %broadcast_clamp_fusion), kind=kCustom, calls=%fused_computation | custom fusion | bytes 49152 | tf_op jit(solution)/shard_map/jit(_take)/gather | solution.py:155
  203.1 4.5 or_and_fusion
  207.9 49.1 %all-to-all-done.2 = bf16[32,128,3,128]{3,1,2,0:T(8,128)(2,1)} async-done(((bf16[32,128,3,128]{3,1,2,0:T(8,128)(2,1)}), bf16[32,128,3,128]{3,1,2,0:T(8,128)(2,1)}, u32[]{:S(2)}, u32[]{:S(2)}) %all-to-all-start.2) | async-done | bytes 3145760 | tf_op jit(solution)/shard_map/all_to_all | solution.py:147
  257.0 2.3 copy.92
  259.4 1.2 fusion
  260.6 2.6 copy-done.2
  263.2 1.2 fusion.3
  264.4 61.4 %all-gather.6.cloned.1.call-done = bf16[4096,3,1,128]{0,3,1,2:T(8,128)(2,1)} async-done(((bf16[128,3,1,128]{0,3,1,2:T(8,128)(2,1)}), bf16[4096,3,1,128]{0,3,1,2:T(8,128)(2,1)}) %all-gather.6.cloned.1.call-update) | async-done | bytes 3145744 | tf_op jit(solution)/shard_map/all_gather | solution.py:150
  325.8 5.3 fusion.23
  331.3 8.7 %all_to_all.72 = bf16[8,16,384]{2,1,0:T(8,128)(2,1)S(1)} all-to-all(bf16[8,16,384]{2,1,0:T(8,128)(2,1)S(1)} %all_to_all.60), channel_id=1, replica_groups=mesh['seq'=8,'blk'=32] {'seq'}, dimensions={0} | all-to-all | bytes 196608 | tf_op jit(solution)/shard_map/all_to_all | solution.py:175
  340.2 19.6 %all_to_all.73 = bf16[16,32,96]{2,0,1:T(8,128)(2,1)S(1)} all-to-all(bf16[16,32,96]{2,0,1:T(8,128)(2,1)S(1)} %copy.101), channel_id=1, replica_groups=mesh['seq'=8,'blk'=32] {'blk'}, dimensions={1} | all-to-all | bytes 196608 | tf_op jit(solution)/shard_map/all_to_all | solution.py:174
  359.9 4.7 fusion.90
  364.5 9.6 %add_convert_fusion = bf16[512,3072]{1,0:T(8,128)(2,1)} fusion(f32[512,3072]{1,0:T(8,128)} %fusion.90, bf16[384,3072]{1,0:T(8,128)(2,1)S(1)} %copy-done, bf16[512,3072]{1,0:T(8,128)(2,1)} %all-gather.4.cloned.1.call-done, bf16[3072,384]{1,0:T(8,128)(2,1)} %param.19), kind=kOutput, calls=%fused_computation.7 | convolution fusion | flops 2420834304 | bytes 17301504 | tf_op jit(solution)/shard_map/dot_general | solution.py:185
  374.2 254.9 %reduce-scatter.2.cloned.1.call-done = bf16[16,3072]{1,0:T(8,128)(2,1)} async-done(((bf16[512,3072]{1,0:T(8,128)(2,1)}), bf16[16,3072]{1,0:T(8,128)(2,1)}) %reduce-scatter.2.cloned.1.call-update) | async-done | bytes 98320 | tf_op jit(solution)/shard_map/reduce_scatter | solution.py:182
  629.0 1.6 fusion.43
  (79 shorter events, 17.9 us)
Async XLA Ops:
  6.5 358.0 %copy-start = (bf16[384,3072]{1,0:T(8,128)(2,1)S(1)}, bf16[384,3072]{1,0:T(8,128)(2,1)}, u32[]{:S(2)}) copy-start(bf16[384,3072]{1,0:T(8,128)(2,1)} %param.23) | copy-start | bytes 7077892
  6.5 7.3 %copy-start.3 = (f32[16,3072]{1,0:T(8,128)S(1)}, f32[16,3072]{1,0:T(8,128)}, u32[]{:S(2)}) copy-start(f32[16,3072]{1,0:T(8,128)} %param.12) | copy-start | bytes 589828
  6.5 110.8 %all-gather.4.cloned.1.call-start = ((), (), s32[]{:S(2)}) async-start(), calls=%async_computation.6 | async-start | bytes 3244032 | tf_op jit(solution)/shard_map/all_gather | solution.py:113
  10.5 4.1 copy-start.11
  14.7 113.3 %copy-start.9 = (f32[128]{0:T(128)S(1)}, f32[128]{0:T(128)}, u32[]{:S(2)}) copy-start(f32[128]{0:T(128)} %param.21) | copy-start | bytes 1540
  14.7 114.1 %copy-start.10 = (f32[128]{0:T(128)S(1)}, f32[128]{0:T(128)}, u32[]{:S(2)}) copy-start(f32[128]{0:T(128)} %param.20) | copy-start | bytes 1540
  121.8 20.5 %all-to-all-start = ((bf16[32,16,288]{2,1,0:T(8,128)(2,1)}), bf16[32,16,288]{2,1,0:T(8,128)(2,1)S(1)}, u32[]{:S(2)}, u32[]{:S(2)}) async-start(bf16[32,16,288]{2,1,0:T(8,128)(2,1)} %bitcast.70), calls=%async_computation | async-start | bytes 786432 | tf_op jit(solution)/shard_map/all_to_all | solution.py:122
  145.3 14.3 %all-to-all-start.1 = ((bf16[16,8,1152]{2,0,1:T(8,128)(2,1)}), bf16[16,8,1152]{2,0,1:T(8,128)(2,1)S(1)}, u32[]{:S(2)}, u32[]{:S(2)}) async-start(bf16[16,8,1152]{2,0,1:T(8,128)(2,1)} %copy.83), calls=%async_computation.1 | async-start | bytes 589824 | tf_op jit(solution)/shard_map/all_to_all | solution.py:121
  159.6 0.7 copy-start.5
  172.0 6.6 %copy-start.6 = (bf16[128,3,1,128]{3,2,1,0:T(2,128)(2,1)S(1)}, bf16[128,3,1,128]{3,2,1,0:T(2,128)(2,1)}, u32[]{:S(2)}) copy-start(bf16[128,3,1,128]{3,2,1,0:T(2,128)(2,1)} %get-tuple-element.5) | copy-start | bytes 294916
  172.0 7.7 %copy-start.1 = (s32[4096]{0:T(1024)S(1)}, s32[4096]{0:T(1024)}, u32[]{:S(2)}) copy-start(s32[4096]{0:T(1024)} %param.13) | copy-start | bytes 49156
  172.0 85.0 %all-to-all-start.2 = ((bf16[32,128,3,128]{3,1,2,0:T(8,128)(2,1)}), bf16[32,128,3,128]{3,1,2,0:T(8,128)(2,1)}, u32[]{:S(2)}, u32[]{:S(2)}) async-start(bf16[32,128,3,128]{3,1,2,0:T(8,128)(2,1)} %stack.9), calls=%async_computation.2 | async-start | bytes 6291456 | tf_op jit(solution)/shard_map/all_to_all | solution.py:147
  178.5 147.2 %all-gather.6.cloned.1.call-start = ((), (), s32[]{:S(2)}) async-start(), calls=%async_computation.8 | async-start | bytes 3244032 | tf_op jit(solution)/shard_map/all_gather | solution.py:150
  179.4 449.7 %reduce-scatter.2.cloned.1.call-start = ((), (), s32[]{:S(2)}) async-start(), calls=%async_computation.7 | async-start | bytes 3244032 | tf_op jit(solution)/shard_map/reduce_scatter | solution.py:182
  179.7 23.1 %copy-start.12 = (s32[4,1]{0,1:T(1,128)S(1)}, s32[4,1]{0,1:T(1,128)}, u32[]{:S(2)}) copy-start(s32[4,1]{0,1:T(1,128)} %copy-done.11) | copy-start | bytes 52
  179.7 27.9 %copy-start.7 = (bf16[128,3,64,1]{0,3,2,1:T(2,128)(2,1)S(1)}, bf16[128,3,64,1]{0,3,2,1:T(2,128)(2,1)}, u32[]{:S(2)}) copy-start(bf16[128,3,64,1]{0,3,2,1:T(2,128)(2,1)} %get-tuple-element.8) | copy-start | bytes 147460
  179.7 27.9 %copy-start.8 = (bf16[128,3,64,1]{0,3,2,1:T(2,128)(2,1)S(1)}, bf16[128,3,64,1]{0,3,2,1:T(2,128)(2,1)}, u32[]{:S(2)}) copy-start(bf16[128,3,64,1]{0,3,2,1:T(2,128)(2,1)} %get-tuple-element.9) | copy-start | bytes 147460
  257.0 2.4 copy-start.4
  260.5 2.7 copy-start.2
Sparse Core Ops, SparseCore 0:
  14.8 102.5 all-gather.3
  182.6 143.1 all-gather.5
  374.3 254.7 reduce-scatter.1
